TPU v7x, 512 devices: a whole 4x8x8 slice. The times are simulated.
512 devices in a mesh: seq: 128 (over z, y, core), head: 4 (over x).
Axes of the slice: x: 4, y: 8, z: 8, core: 2. Of those that a mesh axis runs over, the one named last changes fastest.
Arguments:
- hidden: bfloat16 [16384, 1024], P('seq', 'head'), may hold values from -6 to 6
- queries: bfloat16 [16384, 1024], P('seq', 'head'), may hold values from -40 to 40
- suffix_keys: bfloat16 [16384, 1024], P('seq', 'head'), may hold values from -4 to 4
- suffix_values: bfloat16 [16384, 1024], P('seq', 'head'), may hold values from -6 to 6
- lengths: int32 [128], P('seq'), may hold values from 1 to 128, 10240 in all
- key_cache: bfloat16 [128, 32, 1024], P('seq', None, 'head'), may hold values from -6 to 6
- value_cache: bfloat16 [128, 32, 1024], P('seq', None, 'head'), may hold values from -6 to 6
- page_group: int32 [128], replicated, may hold values from 0 to 3, as said below
- out_weight: bfloat16 [1024, 1024], P('head'), may hold values from -0.1875 to 0.1875
- norm_gain: float32 [1024], replicated, may hold values from 0.1 to 1.9
- router_weight: bfloat16 [1024, 16], P('head'), may hold values from -0.1875 to 0.1875
- routes: int32 [16384, 2], P('seq'), may hold values from 0 to 15, all different within a row; in each aligned block of 16 rows (0 to 15, 16 to 31, ...) at most 2 rows name the same one
- gate_weight: bfloat16 [128, 1024, 2816], P('seq', None, 'head'), as said below
- up_weight: bfloat16 [128, 1024, 2816], P('seq', None, 'head'), as said below
- down_weight: bfloat16 [128, 1024, 2816], P('seq', None, 'head'), as said below
- destinations: int32 [128], replicated, may hold values from 0 to 127, as said below
Outputs:
- layer_output: bfloat16 [16384, 1024], P('seq', 'head')
Inputs may be any that keep to these rules, and one draw needn't show every extreme that they name: `lengths`: the largest length is 128. `page_group`: each of the 4 groups is named by exactly 32 entries. `routes`: each row names 2 different experts; in each aligned block of 16 rows no expert is named by more than 2 rows. `gate_weight`: copies h and h2 with h // 8 == h2 // 8 are equal. `up_weight`: copies h and h2 with h // 8 == h2 // 8 are equal. `down_weight`: copies h and h2 with h // 8 == h2 // 8 are equal. `destinations`: A permutation of the requests in which exactly 32 requests change place.
All inputs are finite; a program needn't handle non-finite values. No bound on the sum of `lengths` on one device may be relied on, other than what follows from the above.
Results may differ from a plain program's by a relative error of at most 0.0065.
Values may be sent and summed in bfloat16 or wider, within the bound.
No kernel may reach another device: no remote copies, remote signals or barrier semaphores. Data moves between devices by JAX's collectives and lax.ppermute only.
A program may use at most 64 MiB of HBM per device.

v0:
```python
import jax
import jax.numpy as jnp
from jax import lax
from jax.sharding import PartitionSpec as P

DH = 64
EXPERTS = 16
TOPK = 2
GROUPS = 4
norm_eps = 1e-06


def page_inverse(page_group, group_pages, groups):
    page_total = page_group.shape[0]
    onehot = (page_group[:, None] == jnp.arange(groups, dtype=jnp.int32)[None, :]).astype(jnp.int32)
    page_rank = jnp.sum((jnp.cumsum(onehot, axis=0) - 1) * onehot, axis=1)
    target = page_group * group_pages + page_rank
    return (
        jnp.zeros((page_total,), jnp.int32).at[target].set(jnp.arange(page_total, dtype=jnp.int32))
    )


def attend_rows(query_rows, key_rows, value_rows, prefix_keys, prefix_values, length, head_total):
    row_count = query_rows.shape[0]
    head_size = query_rows.shape[1] // head_total
    scale = head_size ** (-0.5)

    def heads_of(array):
        return array.reshape(array.shape[0], head_total, head_size)

    prefix_scores = (
        jnp.einsum(
            "qhd,khd->hqk",
            heads_of(query_rows),
            heads_of(prefix_keys),
            preferred_element_type=jnp.float32,
        )
        * scale
    )
    suffix_scores = (
        jnp.einsum(
            "qhd,khd->hqk",
            heads_of(query_rows),
            heads_of(key_rows),
            preferred_element_type=jnp.float32,
        )
        * scale
    )
    query_pos = jnp.arange(row_count, dtype=jnp.int32)[:, None]
    key_pos = jnp.arange(row_count, dtype=jnp.int32)[None, :]
    allowed = (key_pos <= query_pos) & (key_pos < length)
    suffix_scores = jnp.where(allowed[None], suffix_scores, -jnp.inf)
    row_max = jnp.maximum(jnp.max(prefix_scores, axis=2), jnp.max(suffix_scores, axis=2))[..., None]
    prefix_exp = jnp.exp(prefix_scores - row_max)
    suffix_exp = jnp.exp(suffix_scores - row_max)
    denominators = jnp.sum(prefix_exp, axis=2, keepdims=True) + jnp.sum(
        suffix_exp, axis=2, keepdims=True
    )
    prefix_probs = (prefix_exp / denominators).astype(jnp.bfloat16)
    suffix_probs = (suffix_exp / denominators).astype(jnp.bfloat16)
    mixed_heads = jnp.einsum(
        "hqk,khd->qhd", prefix_probs, heads_of(prefix_values), preferred_element_type=jnp.float32
    )
    mixed_heads = mixed_heads + jnp.einsum(
        "hqk,khd->qhd", suffix_probs, heads_of(value_rows), preferred_element_type=jnp.float32
    )
    return mixed_heads.reshape(row_count, head_total * head_size).astype(jnp.bfloat16)


def slot_table(route_rows, replicas, per_device, experts):
    row_count, topk_count = route_rows.shape
    sub_rows = row_count // replicas
    flat_routes = route_rows.reshape(replicas, sub_rows * topk_count)
    onehot = (flat_routes[..., None] == jnp.arange(experts, dtype=jnp.int32)).astype(jnp.int32)
    slot_rank = jnp.sum((jnp.cumsum(onehot, axis=1) - 1) * onehot, axis=2).reshape(-1)
    expert_flat = route_rows.reshape(-1)
    block_of = jnp.arange(row_count * topk_count, dtype=jnp.int32) // (sub_rows * topk_count)
    target_device = expert_flat // per_device * replicas + block_of
    local_slot = expert_flat % per_device
    return (target_device, local_slot, slot_rank)


def on_device(
    hidden,
    queries,
    suffix_keys,
    suffix_values,
    lengths,
    key_cache,
    value_cache,
    page_group,
    out_weight,
    norm_gain,
    router_weight,
    routes,
    gate_weight,
    up_weight,
    down_weight,
    destinations,
):
    seq_count = lax.axis_size("seq")
    head_count = lax.axis_size("head")
    seq_index = lax.axis_index("seq")
    head_index = lax.axis_index("head")
    row_count = hidden.shape[0]
    column_width = hidden.shape[1]
    features = queries.shape[1]
    local_heads = features // DH
    block_devices = seq_count // GROUPS
    page_local = key_cache.shape[0]
    page_rows = key_cache.shape[1]
    group_pages = page_local * block_devices
    replicas = max(1, seq_count // EXPERTS)
    per_device = max(1, EXPERTS // seq_count)
    capacity = 5 * row_count * TOPK // (4 * EXPERTS * replicas)
    inverse = page_inverse(page_group, group_pages, GROUPS)
    group_index = seq_index // block_devices
    half_width = page_rows * features
    local_pages = jnp.concatenate(
        [key_cache.reshape(page_local, half_width), value_cache.reshape(page_local, half_width)],
        axis=1,
    )
    all_pages = lax.all_gather(local_pages, "seq", axis=0, tiled=True)
    chosen = lax.dynamic_slice_in_dim(inverse, group_index * group_pages, group_pages, 0)
    held_pages = jnp.take(all_pages, chosen, axis=0)
    prefix_keys = held_pages[:, :half_width].reshape(group_pages * page_rows, features)
    prefix_values = held_pages[:, half_width:].reshape(group_pages * page_rows, features)
    length = lengths[0]
    attended = attend_rows(
        queries, suffix_keys, suffix_values, prefix_keys, prefix_values, length, local_heads
    )
    partial_proj = jnp.dot(attended, out_weight, preferred_element_type=jnp.float32)
    own_columns = lax.dynamic_slice_in_dim(
        partial_proj, head_index * column_width, column_width, 1
    ) + hidden.astype(jnp.float32)
    partial_proj = lax.dynamic_update_slice_in_dim(
        partial_proj, own_columns, head_index * column_width, 1
    )
    resid = lax.psum(partial_proj, "head")
    normed = (
        resid * lax.rsqrt(jnp.mean(resid * resid, axis=1, keepdims=True) + norm_eps) * norm_gain
    ).astype(jnp.bfloat16)
    normed_columns = lax.dynamic_slice_in_dim(normed, head_index * column_width, column_width, 1)
    logits = lax.psum(
        jnp.dot(normed_columns, router_weight, preferred_element_type=jnp.float32), "head"
    )
    chosen_logits = jnp.take_along_axis(logits, routes, axis=1)
    gate_first = jax.nn.sigmoid(chosen_logits[:, 0] - chosen_logits[:, 1])
    gate_second = jax.nn.sigmoid(chosen_logits[:, 1] - chosen_logits[:, 0])
    target_device, local_slot, slot_rank = slot_table(routes, replicas, per_device, EXPERTS)
    token_index = jnp.arange(row_count * TOPK, dtype=jnp.int32) // TOPK
    send_rows = jnp.zeros((seq_count, per_device, capacity, normed.shape[1]), jnp.bfloat16)
    send_rows = send_rows.at[target_device, local_slot, slot_rank].set(
        jnp.take(normed, token_index, axis=0)
    )
    slots = lax.all_to_all(send_rows, "seq", split_axis=0, concat_axis=0, tiled=True)
    gate_act = jnp.einsum("spnd,pdf->spnf", slots, gate_weight, preferred_element_type=jnp.float32)
    up_act = jnp.einsum("spnd,pdf->spnf", slots, up_weight, preferred_element_type=jnp.float32)
    expert_hidden = (jax.nn.gelu(gate_act, approximate=True) * up_act).astype(jnp.bfloat16)
    partial_out = jnp.einsum(
        "spnf,pdf->spnd", expert_hidden, down_weight, preferred_element_type=jnp.float32
    )
    part_dims = partial_out.shape
    split_part = partial_out.reshape(
        part_dims[0], part_dims[1], part_dims[2], head_count, part_dims[3] // head_count
    )
    arrived = lax.all_to_all(
        lax.all_to_all(
            split_part.astype(jnp.bfloat16), "seq", split_axis=0, concat_axis=0, tiled=True
        ),
        "head",
        split_axis=3,
        concat_axis=3,
        tiled=True,
    ).astype(split_part.dtype)
    returned = jnp.sum(arrived, axis=3).astype(jnp.bfloat16)
    picked = (
        returned[target_device, local_slot, slot_rank]
        .astype(jnp.float32)
        .reshape(row_count, TOPK, column_width)
    )
    resid_columns = lax.dynamic_slice_in_dim(resid, head_index * column_width, column_width, 1)
    layer = resid_columns + gate_first[:, None] * picked[:, 0] + gate_second[:, None] * picked[:, 1]
    layer = layer.astype(jnp.bfloat16)
    live_rows = jnp.arange(row_count, dtype=jnp.int32) < length
    layer = jnp.where(live_rows[:, None], layer, jnp.zeros_like(layer))
    out_pieces = layer.reshape(seq_count, row_count // seq_count, column_width)
    scattered = lax.all_to_all(out_pieces, "seq", split_axis=0, concat_axis=0, tiled=True)
    inverse_destination = (
        jnp.zeros((seq_count,), jnp.int32)
        .at[destinations]
        .set(jnp.arange(seq_count, dtype=jnp.int32))
    )
    reordered = jnp.take(scattered, inverse_destination, axis=0)
    settled = lax.all_to_all(reordered, "seq", split_axis=0, concat_axis=0, tiled=True)
    return settled.reshape(row_count, column_width)


def solution(mesh):
    return jax.shard_map(
        on_device,
        mesh=mesh,
        in_specs=(
            P("seq", "head"),
            P("seq", "head"),
            P("seq", "head"),
            P("seq", "head"),
            P("seq"),
            P("seq", None, "head"),
            P("seq", None, "head"),
            P(),
            P("head", None),
            P(),
            P("head", None),
            P("seq", None),
            P("seq", None, "head"),
            P("seq", None, "head"),
            P("seq", None, "head"),
            P(),
        ),
        out_specs=P("seq", "head"),
        check_vma=False,
    )
```

profile of v0, /device:TPU:1, one launch (start us, length us, event | category | flops | bytes accessed | tf_op | source)
XLA Modules:
  0.0 332.7 jit_solution(16132102906732446111)
XLA Ops:
  6.5 0.9 copy.142
  7.4 0.7 copy.143
  8.1 0.7 maximum_bitcast_fusion
  8.9 0.7 fusion.67
  9.9 0.9 copy.111
  11.5 1.0 copy.113
  12.4 1.6 copy.116
  14.0 0.8 copy.121
  15.0 0.8 select_reduce_fusion
  15.8 1.2 compare_select_fusion.6
  17.0 1.0 scatter_custom_fusion.1
  18.2 0.7 fusion.80
  18.9 1.5 fusion.81
  20.4 83.8 %all-gather.3.cloned.1.call-done = bf16[128,1,16384]{2,1,0:T(2,128)(2,1)} async-done(((bf16[1,1,16384]{2,1,0:T(2,128)(2,1)}), bf16[128,1,16384]{2,1,0:T(2,128)(2,1)}) %all-gather.3.cloned.1.call-update) | async-done | bytes 4194320 | tf_op jit(solution)/shard_map/all_gather | solution.py:123
  104.2 9.9 %copy.185 = bf16[128,1,16384]{2,0,1:T(8,128)(2,1)} copy(bf16[128,1,16384]{2,1,0:T(2,128)(2,1)} %all-gather.3.cloned.1.call-done) | data formatting | bytes 8388608
  114.1 4.8 %gather_fusion = bf16[32,16384]{1,0:T(8,128)(2,1)S(1)} fusion(bf16[128,16384]{1,0:T(8,128)(2,1)} %bitcast.164, s32[1024]{0:T(1024)S(1)} %pad_clamp_fusion.2), kind=kCustom, calls=%fused_computation | custom fusion | bytes 2097280 | tf_op jit(solution)/shard_map/jit(_take)/gather | solution.py:125
  119.1 0.9 fusion.78
  120.0 2.1 reshape_reshape.7
  122.1 1.7 bitcast_reduce_fusion
  123.9 0.9 fusion.1
  125.4 3.3 reshape_reshape.6
  129.4 2.0 convolution_bitcast_fusion.1
  132.3 0.8 copy-done.1
  133.6 47.2 %all-reduce.2.cloned.1.call-done = f32[128,1024]{1,0:T(8,128)} async-done(((f32[128,1024]{1,0:T(8,128)}), f32[128,1024]{1,0:T(8,128)}) %all-reduce.2.cloned.1.call-update) | async-done | bytes 524304 | tf_op jit(solution)/shard_map/psum | solution.py:139
  180.8 1.2 multiply_reduce_fusion
  182.0 1.2 multiply_convert_fusion
  183.1 1.2 gather_fusion.1
  184.7 15.9 %scatter_fusion = bf16[128,2,1024]{2,1,0:T(2,128)(2,1)S(1)} fusion(bf16[128,2,1024]{2,1,0:T(2,128)(2,1)S(1)} %broadcast.370, s32[256]{0:T(256)S(1)} %bitcast.165, bf16[256,1024]{1,0:T(8,128)(2,1)S(1)} %broadcast_select_fusion.1), kind=kCustom, calls=%fused_computation.7 | custom fusion | bytes 1574912 | tf_op jit(solution)/shard_map/scatter | solution.py:153
  200.6 36.9 %all_to_all.25 = bf16[128,1,2,1024]{3,2,1,0:T(2,128)(2,1)S(1)} all-to-all(bf16[128,1,2,1024]{3,2,1,0:T(2,128)(2,1)S(1)} %bitcast.163), channel_id=1, replica_groups=mesh['seq'=128,'head'=4] {'seq'}, dimensions={0} | all-to-all | bytes 1048576 | tf_op jit(solution)/shard_map/all_to_all | solution.py:156
  237.5 2.0 fusion.42
  239.5 3.2 fusion.23
  243.1 1.0 copy.126
  244.0 5.4 %all-to-all-start.1 = ((bf16[128,1,2,4,256]{4,3,2,1,0:T(4,128)(2,1)}), bf16[128,1,2,4,256]{4,3,2,1,0:T(4,128)(2,1)S(1)}, u32[]{:S(2)}, u32[]{:S(2)}) async-start(bf16[128,1,2,4,256]{4,3,2,1,0:T(4,128)(2,1)} %copy.126), calls=%async_computation.1 | async-start | bytes 1048576 | tf_op jit(solution)/shard_map/all_to_all | solution.py:168
  249.7 1.1 scatter_custom_fusion
  251.0 8.1 %psum.15 = f32[128,16]{0,1:T(8,128)S(1)} all-reduce(f32[128,16]{0,1:T(8,128)S(1)} %fusion.65), channel_id=1, replica_groups=mesh['seq'=128,'head'=4] {'head'}, use_global_device_ids=true, to_apply=%region_10.11 | all-reduce | flops 2048 | bytes 16384 | tf_op jit(solution)/shard_map/psum | solution.py:144
  259.1 2.2 gather_fusion.4
  261.5 8.5 %all-to-all-done.1 = bf16[128,1,2,4,256]{4,3,2,1,0:T(4,128)(2,1)S(1)} async-done(((bf16[128,1,2,4,256]{4,3,2,1,0:T(4,128)(2,1)}), bf16[128,1,2,4,256]{4,3,2,1,0:T(4,128)(2,1)S(1)}, u32[]{:S(2)}, u32[]{:S(2)}) %all-to-all-start.1) | async-done | bytes 524320 | tf_op jit(solution)/shard_map/all_to_all | solution.py:168
  270.0 0.9 copy.127
  270.9 3.6 %all-to-all-start.2 = ((bf16[128,1,2,4,256]{4,0,2,1,3:T(8,128)(2,1)}), bf16[128,1,2,4,256]{4,0,2,1,3:T(8,128)(2,1)S(1)}, u32[]{:S(2)}, u32[]{:S(2)}) async-start(bf16[128,1,2,4,256]{4,0,2,1,3:T(8,128)(2,1)} %copy.127), calls=%async_computation.2 | async-start | bytes 1048576 | tf_op jit(solution)/shard_map/all_to_all | solution.py:167
  274.6 9.7 %all-to-all-done.2 = bf16[128,1,2,4,256]{4,0,2,1,3:T(8,128)(2,1)S(1)} async-done(((bf16[128,1,2,4,256]{4,0,2,1,3:T(8,128)(2,1)}), bf16[128,1,2,4,256]{4,0,2,1,3:T(8,128)(2,1)S(1)}, u32[]{:S(2)}, u32[]{:S(2)}) %all-to-all-start.2) | async-done | bytes 524320 | tf_op jit(solution)/shard_map/all_to_all | solution.py:167
  284.5 1.6 gather_fusion.2
  286.5 1.0 fusion.63
  288.1 0.7 reduce.2
  289.5 5.8 %all-to-all-start.3 = ((bf16[128,2,128]{2,1,0:T(2,128)(2,1)}), bf16[128,2,128]{2,1,0:T(2,128)(2,1)S(1)}, u32[]{:S(2)}, u32[]{:S(2)}) async-start(bf16[128,2,128]{2,1,0:T(2,128)(2,1)} %reshape.393), calls=%async_computation.3 | async-start | bytes 131072 | tf_op jit(solution)/shard_map/all_to_all | solution.py:188
  295.3 11.5 %all-to-all-done.3 = bf16[128,2,128]{2,1,0:T(2,128)(2,1)S(1)} async-done(((bf16[128,2,128]{2,1,0:T(2,128)(2,1)}), bf16[128,2,128]{2,1,0:T(2,128)(2,1)S(1)}, u32[]{:S(2)}, u32[]{:S(2)}) %all-to-all-start.3) | async-done | bytes 65568 | tf_op jit(solution)/shard_map/all_to_all | solution.py:188
  306.9 0.8 gather_fusion.3
  307.8 0.7 reduce.3
  308.5 16.7 %all_to_all.26 = bf16[128,2,128]{2,1,0:T(2,128)(2,1)S(1)} all-to-all(bf16[128,2,128]{2,1,0:T(2,128)(2,1)S(1)} %reshape.395), channel_id=1, replica_groups=mesh['seq'=128,'head'=4] {'seq'}, dimensions={0} | all-to-all | bytes 131072 | tf_op jit(solution)/shard_map/all_to_all | solution.py:195
  (86 shorter events, 7.4 us)
Async XLA Ops:
  6.5 233.0 %copy-start = (bf16[1,1024,704]{1,2,0:T(8,128)(2,1)S(1)}, bf16[1,1024,704]{1,2,0:T(8,128)(2,1)}, u32[]{:S(2)}) copy-start(bf16[1,1024,704]{1,2,0:T(8,128)(2,1)} %param.30) | copy-start | bytes 4325380
  6.5 97.7 %all-gather.3.cloned.1.call-start = ((), (), s32[]{:S(2)}) async-start(), calls=%async_computation.6 | async-start | bytes 8454144 | tf_op jit(solution)/shard_map/all_gather | solution.py:123
  8.9 171.9 %all-reduce.2.cloned.1.call-start = ((), (), s32[]{:S(2)}) async-start(), calls=%async_computation.5 | async-start | bytes 1048576 | tf_op jit(solution)/shard_map/psum | solution.py:139
  10.8 103.3 %copy-start.4 = (bf16[128,256]{0,1:T(8,128)(2,1)}, bf16[128,256]{0,1:T(8,128)(2,1)S(1)}, u32[]{:S(2)}) copy-start(bf16[128,256]{0,1:T(8,128)(2,1)S(1)} %copy.111) | copy-start | bytes 196612
  18.0 96.1 %copy-start.14 = (pred[128]{0:T(512)(128)(4,1)}, pred[128]{0:T(512)(128)(4,1)S(1)}, u32[]{:S(2)}) copy-start(pred[128]{0:T(512)(128)(4,1)S(1)} %iota_compare_fusion.4) | copy-start | bytes 388
  122.1 1.7 copy-start.11
  122.1 2.7 copy-start.2
  123.8 1.6 copy-start.8
  129.4 2.0 copy-start.3
  129.4 2.0 copy-start.7
  129.4 2.1 copy-start.9
  129.4 2.3 copy-start.5
  131.4 0.8 copy-start.6
  131.4 1.7 copy-start.10
  131.4 50.6 %copy-start.13 = (f32[1024]{0:T(1024)S(1)}, f32[1024]{0:T(1024)}, u32[]{:S(2)}) copy-start(f32[1024]{0:T(1024)} %param.25) | copy-start | bytes 12292
  132.3 0.8 copy-start.1
  242.7 8.2 %copy-start.12 = (bf16[256,16]{0,1:T(8,128)(2,1)S(1)}, bf16[256,16]{0,1:T(8,128)(2,1)}, u32[]{:S(2)}) copy-start(bf16[256,16]{0,1:T(8,128)(2,1)} %param.26) | copy-start | bytes 24580
  244.0 26.0 %all-to-all-start.1 = ((bf16[128,1,2,4,256]{4,3,2,1,0:T(4,128)(2,1)}), bf16[128,1,2,4,256]{4,3,2,1,0:T(4,128)(2,1)S(1)}, u32[]{:S(2)}, u32[]{:S(2)}) async-start(bf16[128,1,2,4,256]{4,3,2,1,0:T(4,128)(2,1)} %copy.126), calls=%async_computation.1 | async-start | bytes 1048576 | tf_op jit(solution)/shard_map/all_to_all | solution.py:168
  270.9 15.5 %copy-start.15 = (pred[128]{0:T(512)(128)(4,1)S(1)}, pred[128]{0:T(512)(128)(4,1)}, u32[]{:S(2)}) copy-start(pred[128]{0:T(512)(128)(4,1)} %copy-done.14) | copy-start | bytes 388
  270.9 13.3 %all-to-all-start.2 = ((bf16[128,1,2,4,256]{4,0,2,1,3:T(8,128)(2,1)}), bf16[128,1,2,4,256]{4,0,2,1,3:T(8,128)(2,1)S(1)}, u32[]{:S(2)}, u32[]{:S(2)}) async-start(bf16[128,1,2,4,256]{4,0,2,1,3:T(8,128)(2,1)} %copy.127), calls=%async_computation.2 | async-start | bytes 1048576 | tf_op jit(solution)/shard_map/all_to_all | solution.py:167
  289.5 17.3 %all-to-all-start.3 = ((bf16[128,2,128]{2,1,0:T(2,128)(2,1)}), bf16[128,2,128]{2,1,0:T(2,128)(2,1)S(1)}, u32[]{:S(2)}, u32[]{:S(2)}) async-start(bf16[128,2,128]{2,1,0:T(2,128)(2,1)} %reshape.393), calls=%async_computation.3 | async-start | bytes 131072 | tf_op jit(solution)/shard_map/all_to_all | solution.py:188
Sparse Core Ops, SparseCore 0:
  10.5 93.6 all-gather.2
  133.2 47.5 all-reduce.1
where the time goes:
time: 334 us; the launch traced here: 333 us
  waiting for transfers between devices  161 us (48%)
  blocking collectives  61.7 us (18%)
  local copies, waits for them, and re-layouts  57.8 us (17%)
  starting transfers between devices  14.9 us (4%)
  between operations  14.6 us (4%)
  other arithmetic  12.1 us (4%)
  matrix products  10.9 us (3%)
    all_gather x1, waiting for transfers between devices, on_device(): all_pages = lax.all_gather(local_pages, 'seq', axis=0, tiled=True)  83.8 us
    psum x1, waiting for transfers between devices, on_device(): resid = lax.psum(partial_proj, 'head')  47.2 us
    all_to_all x1, blocking collectives, on_device(): lax.all_to_all(send_rows, 'seq', split_axis=0, concat_axis=0, tiled=True)  36.9 us
    unnamed x45, local copies, waits for them, and re-layouts  18.3 us
    all_to_all x1, blocking collectives, on_device(): lax.all_to_all(reordered, 'seq', split_axis=0, concat_axis=0, tiled=True)  16.7 us
    scatter x1, local copies, waits for them, and re-layouts, on_device(): send_rows.at[target_device, local_slot, slot_rank]  15.9 us
    all_to_all x1, waiting for transfers between devices, on_device(): lax.all_to_all(out_pieces, 'seq', split_axis=0, concat_axis=0, tiled=True)  11.5 us
    all_to_all x1, waiting for transfers between devices, on_device(): lax.all_to_all(lax.all_to_all(split_part.astype(jnp.bfloat16), 'seq', spl...  9.7 us
  transfers between devices with their start and end apart: 5, of which 5 were waited for; matrix products, arithmetic and copies ran while one was open for 5% of the time, Pallas kernels for 0%

commit v1 on v0

--- a/solution.py
+++ b/solution.py
@@ -136,7 +136,9 @@
     partial_proj = lax.dynamic_update_slice_in_dim(
         partial_proj, own_columns, head_index * column_width, 1
     )
-    resid = lax.psum(partial_proj, "head")
+    resid = partial_proj
+    for hop in (1, 2):
+        resid = resid + lax.ppermute(resid, "head", [(dev, dev ^ hop) for dev in range(4)])
     normed = (
         resid * lax.rsqrt(jnp.mean(resid * resid, axis=1, keepdims=True) + norm_eps) * norm_gain
     ).astype(jnp.bfloat16)

time: 334 us -> 307 us (0.919)
  waiting for transfers between devices: 161 us -> 136 us
  starting transfers between devices: 14.9 us -> 23.3 us
  blocking collectives: 61.7 us -> 56.9 us
  other arithmetic: 12.1 us -> 7.4 us
    psum x1 -> x0, waiting for transfers between devices: 47.2 us -> none  [on_device(): resid = lax.psum(partial_proj, 'head')]
    ppermute x0 -> x2, waiting for transfers between devices: none -> 21.5 us  [on_device(): lax.ppermute(resid, 'head', [(dev, dev ^ hop) for dev in range(4)])]
    ppermute x0 -> x2, starting transfers between devices: none -> 7.89 us  [on_device(): lax.ppermute(resid, 'head', [(dev, dev ^ hop) for dev in range(4)])]
    all_to_all x1, blocking collectives: 36.9 us -> 31.1 us  [on_device(): lax.all_to_all(send_rows, 'seq', split_axis=0, concat_axis=0, tiled=True)]
    unnamed x45 -> x33, local copies, waits for them, and re-layouts: 18.3 us -> 16.8 us
  transfers between devices with their start and end apart: 5 -> 6, of which waited for: 5 -> 6; matrix products, arithmetic and copies ran while one was open for 5% -> 4% of each run, Pallas kernels for 0% -> 0%
where the time goes in v1:
time: 307 us; the launch traced here: 306 us
  waiting for transfers between devices  136 us (44%)
  blocking collectives  56.9 us (19%)
  local copies, waits for them, and re-layouts  56.1 us (18%)
  starting transfers between devices  23.3 us (8%)
  between operations  14.5 us (5%)
  matrix products  11.4 us (4%)
  other arithmetic  7.4 us (2%)
    all_gather x1, waiting for transfers between devices, on_device(): all_pages = lax.all_gather(local_pages, 'seq', axis=0, tiled=True)  86 us
    all_to_all x1, blocking collectives, on_device(): lax.all_to_all(send_rows, 'seq', split_axis=0, concat_axis=0, tiled=True)  31.1 us
    ppermute x2, waiting for transfers between devices, on_device(): lax.ppermute(resid, 'head', [(dev, dev ^ hop) for dev in range(4)])  21.5 us
    unnamed x33, local copies, waits for them, and re-layouts  16.8 us
    all_to_all x1, blocking collectives, on_device(): lax.all_to_all(reordered, 'seq', split_axis=0, concat_axis=0, tiled=True)  16.7 us
    scatter x1, local copies, waits for them, and re-layouts, on_device(): send_rows.at[target_device, local_slot, slot_rank]  15.9 us
    all_to_all x1, waiting for transfers between devices, on_device(): lax.all_to_all(out_pieces, 'seq', split_axis=0, concat_axis=0, tiled=True)  11.5 us
    all_to_all x1, waiting for transfers between devices, on_device(): lax.all_to_all(lax.all_to_all(split_part.astype(jnp.bfloat16), 'seq', spl...  9.52 us
  transfers between devices with their start and end apart: 6, of which 6 were waited for; matrix products, arithmetic and copies ran while one was open for 4% of the time, Pallas kernels for 0%

profile of v1, /device:TPU:1, one launch (start us, length us, event | category | flops | bytes accessed | tf_op | source)
XLA Modules:
  0.0 305.9 jit_solution(3304283626580576685)
XLA Ops:
  6.5 0.9 copy.142
  7.4 0.7 copy.143
  8.1 0.7 maximum_bitcast_fusion
  8.9 0.7 fusion.67
  9.8 0.9 copy.111
  11.4 1.0 copy.113
  12.4 1.6 copy.116
  14.0 0.8 select_reduce_fusion
  14.8 1.3 compare_select_fusion.6
  16.0 1.0 scatter_custom_fusion.1
  17.2 0.9 fusion.81
  18.2 86.0 %all-gather.3.cloned.1.call-done = bf16[128,1,16384]{2,1,0:T(2,128)(2,1)} async-done(((bf16[1,1,16384]{2,1,0:T(2,128)(2,1)}), bf16[128,1,16384]{2,1,0:T(2,128)(2,1)}) %all-gather.3.cloned.1.call-update) | async-done | bytes 4194320 | tf_op jit(solution)/shard_map/all_gather | solution.py:123
  104.2 9.9 %copy.185 = bf16[128,1,16384]{2,0,1:T(8,128)(2,1)} copy(bf16[128,1,16384]{2,1,0:T(2,128)(2,1)} %all-gather.3.cloned.1.call-done) | data formatting | bytes 8388608
  114.1 4.8 %gather_fusion = bf16[32,16384]{1,0:T(8,128)(2,1)S(1)} fusion(bf16[128,16384]{1,0:T(8,128)(2,1)} %bitcast.164, s32[1024]{0:T(1024)S(1)} %pad_clamp_fusion.2), kind=kCustom, calls=%fused_computation | custom fusion | bytes 2097280 | tf_op jit(solution)/shard_map/jit(_take)/gather | solution.py:125
  119.1 0.9 fusion.78
  120.0 2.1 reshape_reshape.7
  122.1 1.7 bitcast_reduce_fusion
  124.3 3.3 %reshape_reshape.6 = bf16[1024,4,64]{2,1,0:T(4,128)(2,1)} reshape(bf16[32,8192]{1,0:T(8,128)(2,1)} %get-tuple-element.12) | data formatting | bytes 1048576 | tf_op jit(solution)/shard_map/reshape;reshape | solution.py:29
  127.5 2.0 convolution_bitcast_fusion.1
  130.4 3.3 %collective-permute-start = (f32[128,1024]{1,0:T(8,128)S(1)}, f32[128,1024]{1,0:T(8,128)S(1)}, u32[]{:S(2)}, u32[]{:S(2)}) collective-permute-start(f32[128,1024]{1,0:T(8,128)S(1)} %add_dynamic-update-slice_fusion), channel_id=1, source_target_pairs={{0,1},{1,0},{2,3},{3,2},{4,5},{5,4},{6,7},{7,6},{8,9},{9,8},{10,11... | collective-permute-start | bytes 1572872 | tf_op jit(solution)/shard_map/ppermute | solution.py:141
  134.0 0.7 fusion.80
  134.7 10.8 %collective-permute-done = f32[128,1024]{1,0:T(8,128)S(1)} collective-permute-done((f32[128,1024]{1,0:T(8,128)S(1)}, f32[128,1024]{1,0:T(8,128)S(1)}, u32[]{:S(2)}, u32[]{:S(2)}) %collective-permute-start) | collective-permute-done | bytes 524320 | tf_op jit(solution)/shard_map/ppermute | solution.py:141
  145.6 4.6 %collective-permute-start.1 = (f32[128,1024]{1,0:T(8,128)S(1)}, f32[128,1024]{1,0:T(8,128)S(1)}, u32[]{:S(2)}, u32[]{:S(2)}) collective-permute-start(f32[128,1024]{1,0:T(8,128)S(1)} %add.187), channel_id=1, source_target_pairs={{0,2},{1,3},{2,0},{3,1},{4,6},{5,7},{6,4},{7,5},{8,10},{9,11},{10,... | collective-permute-start | bytes 1572872 | tf_op jit(solution)/shard_map/ppermute | solution.py:141
  150.7 10.7 %collective-permute-done.1 = f32[128,1024]{1,0:T(8,128)S(1)} collective-permute-done((f32[128,1024]{1,0:T(8,128)S(1)}, f32[128,1024]{1,0:T(8,128)S(1)}, u32[]{:S(2)}, u32[]{:S(2)}) %collective-permute-start.1) | collective-permute-done | bytes 524320 | tf_op jit(solution)/shard_map/ppermute | solution.py:141
  161.6 1.2 gather_fusion.1
  163.2 15.9 %scatter_fusion = bf16[128,2,1024]{2,1,0:T(2,128)(2,1)S(1)} fusion(bf16[128,2,1024]{2,1,0:T(2,128)(2,1)S(1)} %broadcast.370, s32[256]{0:T(256)S(1)} %bitcast.165, bf16[256,1024]{1,0:T(8,128)(2,1)S(1)} %broadcast_select_fusion.1), kind=kCustom, calls=%fused_computation.7 | custom fusion | bytes 1574912 | tf_op jit(solution)/shard_map/scatter | solution.py:155
  179.1 31.1 %all_to_all.25 = bf16[128,1,2,1024]{3,2,1,0:T(2,128)(2,1)S(1)} all-to-all(bf16[128,1,2,1024]{3,2,1,0:T(2,128)(2,1)S(1)} %bitcast.163), channel_id=1, replica_groups=mesh['seq'=128,'head'=4] {'seq'}, dimensions={0} | all-to-all | bytes 1048576 | tf_op jit(solution)/shard_map/all_to_all | solution.py:158
  210.2 2.9 fusion.42
  213.0 3.3 %fusion.23 = bf16[128,1,2,1024]{3,0,2,1:T(8,128)(2,1)S(1)} fusion(bf16[1,1024,704]{1,2,0:T(8,128)(2,1)S(1)} %copy-done, f32[128,1,2,704]{0,3,2,1:T(8,128)} %fusion.42, bf16[1,1024,704]{1,2,0:T(8,128)(2,1)} %param.29, bf16[128,1,2,1024]{3,2,1,0:T(2,128)(2,1)S(1)} %all_to_all.25), kind=kOutput, calls=%fused_computation.25 | convolution fusion | flops 738820096 | bytes 4653056 | tf_op jit(solution)/shard_map/spnf,pdf->spnd/dot_general | solution.py:162
  216.8 1.0 copy.126
  217.7 5.4 %all-to-all-start.1 = ((bf16[128,1,2,4,256]{4,3,2,1,0:T(4,128)(2,1)}), bf16[128,1,2,4,256]{4,3,2,1,0:T(4,128)(2,1)S(1)}, u32[]{:S(2)}, u32[]{:S(2)}) async-start(bf16[128,1,2,4,256]{4,3,2,1,0:T(4,128)(2,1)} %copy.126), calls=%async_computation.1 | async-start | bytes 1048576 | tf_op jit(solution)/shard_map/all_to_all | solution.py:170
  223.4 1.1 scatter_custom_fusion
  224.7 9.1 %psum.7 = f32[128,16]{0,1:T(8,128)S(1)} all-reduce(f32[128,16]{0,1:T(8,128)S(1)} %fusion.65), channel_id=1, replica_groups=mesh['seq'=128,'head'=4] {'head'}, use_global_device_ids=true, to_apply=%region_9.10 | all-reduce | flops 2048 | bytes 16384 | tf_op jit(solution)/shard_map/psum | solution.py:146
  233.8 2.0 gather_fusion.4
  236.0 7.7 %all-to-all-done.1 = bf16[128,1,2,4,256]{4,3,2,1,0:T(4,128)(2,1)S(1)} async-done(((bf16[128,1,2,4,256]{4,3,2,1,0:T(4,128)(2,1)}), bf16[128,1,2,4,256]{4,3,2,1,0:T(4,128)(2,1)S(1)}, u32[]{:S(2)}, u32[]{:S(2)}) %all-to-all-start.1) | async-done | bytes 524320 | tf_op jit(solution)/shard_map/all_to_all | solution.py:170
  243.7 0.9 copy.127
  244.6 4.0 %all-to-all-start.2 = ((bf16[128,1,2,4,256]{4,0,2,1,3:T(8,128)(2,1)}), bf16[128,1,2,4,256]{4,0,2,1,3:T(8,128)(2,1)S(1)}, u32[]{:S(2)}, u32[]{:S(2)}) async-start(bf16[128,1,2,4,256]{4,0,2,1,3:T(8,128)(2,1)} %copy.127), calls=%async_computation.2 | async-start | bytes 1048576 | tf_op jit(solution)/shard_map/all_to_all | solution.py:169
  248.6 9.5 %all-to-all-done.2 = bf16[128,1,2,4,256]{4,0,2,1,3:T(8,128)(2,1)S(1)} async-done(((bf16[128,1,2,4,256]{4,0,2,1,3:T(8,128)(2,1)}), bf16[128,1,2,4,256]{4,0,2,1,3:T(8,128)(2,1)S(1)}, u32[]{:S(2)}, u32[]{:S(2)}) %all-to-all-start.2) | async-done | bytes 524320 | tf_op jit(solution)/shard_map/all_to_all | solution.py:169
  258.3 1.6 gather_fusion.2
  260.4 0.6 broadcast.440
  261.0 0.7 reduce.2
  261.7 0.7 reshape.393
  262.4 6.0 %all-to-all-start.3 = ((bf16[128,2,128]{2,1,0:T(2,128)(2,1)}), bf16[128,2,128]{2,1,0:T(2,128)(2,1)S(1)}, u32[]{:S(2)}, u32[]{:S(2)}) async-start(bf16[128,2,128]{2,1,0:T(2,128)(2,1)} %reshape.393), calls=%async_computation.3 | async-start | bytes 131072 | tf_op jit(solution)/shard_map/all_to_all | solution.py:190
  268.4 11.5 %all-to-all-done.3 = bf16[128,2,128]{2,1,0:T(2,128)(2,1)S(1)} async-done(((bf16[128,2,128]{2,1,0:T(2,128)(2,1)}), bf16[128,2,128]{2,1,0:T(2,128)(2,1)S(1)}, u32[]{:S(2)}, u32[]{:S(2)}) %all-to-all-start.3) | async-done | bytes 65568 | tf_op jit(solution)/shard_map/all_to_all | solution.py:190
  280.0 0.8 gather_fusion.3
  280.9 0.7 reduce.3
  281.7 16.7 %all_to_all.26 = bf16[128,2,128]{2,1,0:T(2,128)(2,1)S(1)} all-to-all(bf16[128,2,128]{2,1,0:T(2,128)(2,1)S(1)} %reshape.395), channel_id=1, replica_groups=mesh['seq'=128,'head'=4] {'seq'}, dimensions={0} | all-to-all | bytes 131072 | tf_op jit(solution)/shard_map/all_to_all | solution.py:197
  298.4 0.6 copy.187
  (76 shorter events, 5.1 us)
Async XLA Ops:
  6.5 206.5 %copy-start = (bf16[1,1024,704]{1,2,0:T(8,128)(2,1)S(1)}, bf16[1,1024,704]{1,2,0:T(8,128)(2,1)}, u32[]{:S(2)}) copy-start(bf16[1,1024,704]{1,2,0:T(8,128)(2,1)} %param.30) | copy-start | bytes 4325380
  6.5 97.7 %all-gather.3.cloned.1.call-start = ((), (), s32[]{:S(2)}) async-start(), calls=%async_computation.5 | async-start | bytes 8454144 | tf_op jit(solution)/shard_map/all_gather | solution.py:123
  10.8 103.3 %copy-start.3 = (bf16[128,256]{0,1:T(8,128)(2,1)}, bf16[128,256]{0,1:T(8,128)(2,1)S(1)}, u32[]{:S(2)}) copy-start(bf16[128,256]{0,1:T(8,128)(2,1)S(1)} %copy.111) | copy-start | bytes 196612
  122.1 2.1 copy-start.1
  127.5 2.0 copy-start.2
  127.5 2.0 copy-start.6
  127.5 2.2 copy-start.4
  129.5 0.8 copy-start.5
  129.5 4.1 %copy-start.7 = (s32[128,2]{0,1:T(2,128)S(1)}, s32[128,2]{0,1:T(2,128)}, u32[]{:S(2)}) copy-start(s32[128,2]{0,1:T(2,128)} %param.27) | copy-start | bytes 3076
  130.4 31.1 %copy-start.9 = (f32[1024]{0:T(1024)S(1)}, f32[1024]{0:T(1024)}, u32[]{:S(2)}) copy-start(f32[1024]{0:T(1024)} %param.25) | copy-start | bytes 12292
  130.4 15.1 %collective-permute-start = (f32[128,1024]{1,0:T(8,128)S(1)}, f32[128,1024]{1,0:T(8,128)S(1)}, u32[]{:S(2)}, u32[]{:S(2)}) collective-permute-start(f32[128,1024]{1,0:T(8,128)S(1)} %add_dynamic-update-slice_fusion), channel_id=1, source_target_pairs={{0,1},{1,0},{2,3},{3,2},{4,5},{5,4},{6,7},{7,6},{8,9},{9,8},{10,11... | collective-permute-start | bytes 1572872 | tf_op jit(solution)/shard_map/ppermute | solution.py:141
  145.6 15.7 %collective-permute-start.1 = (f32[128,1024]{1,0:T(8,128)S(1)}, f32[128,1024]{1,0:T(8,128)S(1)}, u32[]{:S(2)}, u32[]{:S(2)}) collective-permute-start(f32[128,1024]{1,0:T(8,128)S(1)} %add.187), channel_id=1, source_target_pairs={{0,2},{1,3},{2,0},{3,1},{4,6},{5,7},{6,4},{7,5},{8,10},{9,11},{10,... | collective-permute-start | bytes 1572872 | tf_op jit(solution)/shard_map/ppermute | solution.py:141
  216.4 8.2 %copy-start.8 = (bf16[256,16]{0,1:T(8,128)(2,1)S(1)}, bf16[256,16]{0,1:T(8,128)(2,1)}, u32[]{:S(2)}) copy-start(bf16[256,16]{0,1:T(8,128)(2,1)} %param.26) | copy-start | bytes 24580
  217.7 26.0 %all-to-all-start.1 = ((bf16[128,1,2,4,256]{4,3,2,1,0:T(4,128)(2,1)}), bf16[128,1,2,4,256]{4,3,2,1,0:T(4,128)(2,1)S(1)}, u32[]{:S(2)}, u32[]{:S(2)}) async-start(bf16[128,1,2,4,256]{4,3,2,1,0:T(4,128)(2,1)} %copy.126), calls=%async_computation.1 | async-start | bytes 1048576 | tf_op jit(solution)/shard_map/all_to_all | solution.py:170
  244.6 13.5 %all-to-all-start.2 = ((bf16[128,1,2,4,256]{4,0,2,1,3:T(8,128)(2,1)}), bf16[128,1,2,4,256]{4,0,2,1,3:T(8,128)(2,1)S(1)}, u32[]{:S(2)}, u32[]{:S(2)}) async-start(bf16[128,1,2,4,256]{4,0,2,1,3:T(8,128)(2,1)} %copy.127), calls=%async_computation.2 | async-start | bytes 1048576 | tf_op jit(solution)/shard_map/all_to_all | solution.py:169
  262.4 17.6 %all-to-all-start.3 = ((bf16[128,2,128]{2,1,0:T(2,128)(2,1)}), bf16[128,2,128]{2,1,0:T(2,128)(2,1)S(1)}, u32[]{:S(2)}, u32[]{:S(2)}) async-start(bf16[128,2,128]{2,1,0:T(2,128)(2,1)} %reshape.393), calls=%async_computation.3 | async-start | bytes 131072 | tf_op jit(solution)/shard_map/all_to_all | solution.py:190
Sparse Core Ops, SparseCore 0:
  10.5 93.6 all-gather.2
